TPU v7x, 256 devices: a whole 4x4x8 slice. The times are simulated.
256 devices in a mesh: grp: 8 (over x, core), dev: 32 (over z, y).
Axes of the slice: x: 4, y: 4, z: 8, core: 2. Of those that a mesh axis runs over, the one named last changes fastest.
Arguments:
- references: bfloat16 [192, 2048], P('dev'), may hold values from -4 to 4
- particles: bfloat16 [2048, 65536], P(None, ('grp', 'dev')), may hold values from -1300 to 1300
- defocus_bin: int32 [65536], P(('grp', 'dev')), may hold values from 0 to 63
- contrast_table: float32 [64, 32], replicated, may hold values from 0.1 to 1
- noise_power: float32 [32], replicated, may hold values from 300 to 3000
- class_prior: float32 [192], replicated, may hold values from -3 to 3
Outputs:
- new_references: float32 [192, 2048], P('dev')
- occupancy: float32 [192], P('dev')
All inputs are finite; a program needn't handle non-finite values.
Results may differ from a plain program's by a relative error of at most 0.0015.
Values may be sent and summed in bfloat16 or wider, within the bound.
No kernel may reach another device: no remote copies, remote signals or barrier semaphores. Data moves between devices by JAX's collectives and lax.ppermute only.
A program may use at most 64 MiB of HBM per device.

v0:
```python
import math
import jax
import jax.numpy as jnp
from jax import lax
from jax.sharding import PartitionSpec as P

Q = 32
M = 32
R = 128
CLS_DEV = 6


def angle_tables(cycle_freqs, count_turns):
    freq_index = jnp.arange(cycle_freqs, dtype=jnp.int32)
    turn_index = jnp.arange(count_turns, dtype=jnp.int32)
    wrapped = freq_index[:, None] * turn_index[None, :] % count_turns
    phases = 2.0 * math.pi / count_turns * wrapped.astype(jnp.float32)
    factor = jnp.where(freq_index == 0, 1.0, 2.0).astype(jnp.float32)[:, None]
    cosine = jnp.cos(phases)
    sine_part = jnp.sin(phases)
    score_table = jnp.stack([factor * cosine, factor * sine_part], 0).astype(jnp.bfloat16)
    turn_table = jnp.stack([cosine, sine_part], 0).astype(jnp.bfloat16)
    return (score_table, turn_table)


def particle_terms(particles, defocus_bin, contrast_table, noise_power):
    columns = particles.shape[1]
    cycle_count = contrast_table.shape[1]
    freq_count = particles.shape[0] // (2 * cycle_count)
    onehot = (
        defocus_bin[None, :] == jnp.arange(contrast_table.shape[0], dtype=jnp.int32)[:, None]
    ).astype(jnp.float32)
    contrast = jnp.dot(contrast_table.T, onehot, precision=lax.Precision.HIGHEST)
    scaled = contrast / noise_power[:, None]
    power_term = contrast * scaled
    weighted = (
        particles.astype(jnp.float32).reshape(freq_count, 2, cycle_count, columns)
        * scaled[None, None]
    ).astype(jnp.bfloat16)
    return (weighted.reshape(freq_count, 2 * cycle_count, columns), power_term)


def class_rows(class_block):
    classes = class_block.shape[0]
    class_grid = class_block.reshape(classes, M, 2, Q)
    real_part = class_grid[:, :, 0, :]
    imag_part = class_grid[:, :, 1, :]
    rows_real = jnp.concatenate([real_part, imag_part], -1)
    rows_imag = jnp.concatenate([-imag_part, real_part], -1)
    stacked = jnp.stack([rows_real, rows_imag], 0)
    factor = jnp.where(jnp.arange(M) == 0, 1.0, 2.0).astype(jnp.float32)
    squares = class_grid.astype(jnp.float32) ** 2
    cycle_power = jnp.sum(jnp.sum(squares, axis=2) * factor[None, :, None], axis=1)
    return (stacked, cycle_power)


def block_rows(total_rows):
    return CLS_DEV * math.gcd(total_rows // CLS_DEV, 4)


def local(references, particles, defocus_bin, contrast_table, noise_power, class_prior):
    weighted, power_term = particle_terms(particles, defocus_bin, contrast_table, noise_power)
    score_table, turn_table = angle_tables(M, R)
    columns = particles.shape[1]
    classes_total = CLS_DEV * lax.axis_size("dev")

    def block_scores(class_block, first_row):
        stacked, cycle_power = class_rows(class_block)
        prior_part = lax.dynamic_slice_in_dim(class_prior, first_row, class_block.shape[0], 0)
        crossed = jnp.einsum(
            "pkmc,mcb->pmkb", stacked, weighted, preferred_element_type=jnp.float32
        ).astype(jnp.bfloat16)
        scores = jnp.einsum(
            "pmkb,pmr->krb", crossed, score_table, preferred_element_type=jnp.float32
        )
        penalty = jnp.dot(cycle_power, power_term, precision=lax.Precision.HIGHEST)
        return scores - 0.5 * penalty[:, None, :] + prior_part[:, None, None]

    initial = (jnp.full((columns,), -1e30, jnp.float32), jnp.zeros((columns,), jnp.float32))
    empty_sums = (
        jnp.zeros((classes_total, 2 * M * Q), jnp.float32),
        jnp.zeros((classes_total, Q), jnp.float32),
        jnp.zeros((classes_total,), jnp.float32),
    )
    gathered = lax.all_gather(references, "dev", axis=0, tiled=True)
    height = block_rows(gathered.shape[0])
    block_count = gathered.shape[0] // height
    blocks = gathered.reshape(block_count, height, gathered.shape[1])

    def one_block(current, block_item):
        class_block, offset = block_item
        scores = block_scores(class_block, offset * height)
        block_max = jnp.max(scores, axis=(0, 1))
        new_max = jnp.maximum(current[0], block_max)
        block_total = jnp.sum(jnp.exp(scores - new_max[None, None, :]), axis=(0, 1))
        return ((new_max, current[1] * jnp.exp(current[0] - new_max) + block_total), None)

    result, unused = lax.scan(
        one_block, initial, (blocks, jnp.arange(block_count, dtype=jnp.int32))
    )
    log_norm = result[0] + jnp.log(result[1])
    add_height = block_rows(gathered.shape[0])
    block_count = gathered.shape[0] // add_height
    blocks = gathered.reshape(block_count, add_height, gathered.shape[1])

    def one_block(current, block_item):
        class_block, offset = block_item
        row_start = offset * add_height
        scores = block_scores(class_block, row_start)
        responsibility = jnp.exp(scores - log_norm[None, None, :]).astype(jnp.bfloat16)
        spectra = jnp.einsum(
            "krb,pmr->pmkb", responsibility, turn_table, preferred_element_type=jnp.float32
        ).astype(jnp.bfloat16)
        products = jnp.einsum(
            "pmkb,mcb->kpmc", spectra, weighted, preferred_element_type=jnp.float32
        )
        real_sum = products[:, 0, :, :Q] + products[:, 1, :, Q:]
        imag_sum = products[:, 0, :, Q:] - products[:, 1, :, :Q]
        numerator = jnp.stack([real_sum, imag_sum], 2).reshape(add_height, 2 * M * Q)
        class_weight = jnp.sum(responsibility.astype(jnp.float32), axis=1)
        cycle_sum = jnp.dot(class_weight, power_term.T, precision=lax.Precision.HIGHEST)
        class_mass = jnp.sum(class_weight, axis=1)
        updated = (
            lax.dynamic_update_slice_in_dim(current[0], numerator, row_start, 0),
            lax.dynamic_update_slice_in_dim(current[1], cycle_sum, row_start, 0),
            lax.dynamic_update_slice_in_dim(current[2], class_mass, row_start, 0),
        )
        return (updated, None)

    result, unused = lax.scan(
        one_block, empty_sums, (blocks, jnp.arange(block_count, dtype=jnp.int32))
    )
    numer_all, cycles_all, mass_all = result
    merged = lax.psum((numer_all, cycles_all, mass_all), ("grp", "dev"))
    own_start = lax.axis_index("dev") * CLS_DEV
    numerator = lax.dynamic_slice_in_dim(merged[0], own_start, CLS_DEV, 0)
    cycle_sum = lax.dynamic_slice_in_dim(merged[1], own_start, CLS_DEV, 0)
    class_mass = lax.dynamic_slice_in_dim(merged[2], own_start, CLS_DEV, 0)
    new_references = (numerator.reshape(CLS_DEV, M, 2, Q) / cycle_sum[:, None, None, :]).reshape(
        CLS_DEV, 2 * M * Q
    )
    particle_total = columns * lax.axis_size("grp") * lax.axis_size("dev")
    occupancy = class_mass * (classes_total / particle_total)
    return (new_references, occupancy)


def solution(mesh):
    return jax.shard_map(
        local,
        mesh=mesh,
        in_specs=(P("dev", None), P(None, ("grp", "dev")), P(("grp", "dev")), P(), P(), P()),
        out_specs=(P("dev", None), P("dev")),
        check_vma=False,
    )
```

profile of v0, /device:TPU:2, one launch (start us, length us, event | category | flops | bytes accessed | tf_op | source)
XLA Modules:
  0.0 525.7 jit_solution(9444845568496355798)
XLA Ops:
  7.5 53.8 %all-gather = bf16[32,6,2048]{2,1,0:T(8,128)(2,1)S(1)} all-gather(bf16[1,6,2048]{2,1,0:T(8,128)(2,1)} %bitcast.179), channel_id=1, replica_groups=mesh['grp'=8,'dev'=32] {'dev'}, dimensions={0}, use_global_device_ids=true | all-gather | bytes 811008 | tf_op jit(solution)/shard_map/all_gather | solution.py:85
  61.2 1.2 reshape.224
  63.3 1.2 fusion.39
  64.5 87.8 %while.28 = (s32[]{:T(128)}, f32[256]{0:T(256)S(1)}, f32[256]{0:T(256)S(1)}, bf16[8,24,2048]{2,1,0:T(8,128)(2,1)}, bf16[32,64,256]{2,1,0:T(8,128)(2,1)}, /*index...) while((s32[]{:T(128)}, f32[256]{0:T(256)S(1)}, ...), condition=%wide.region_5.6_spmd.clone, body=%wide.region_0.5_spmd.clone.sunk | while | flops 159947328 | bytes 10727242 | solution.py:98
  67.3 2.5 fusion.111
  71.1 1.2 multiply_reduce_fusion.10
  72.5 2.0 fusion.112
  78.3 2.5 fusion.111
  82.0 1.2 multiply_reduce_fusion.10
  83.5 2.0 fusion.112
  89.2 2.5 fusion.111
  93.0 1.2 multiply_reduce_fusion.10
  94.5 2.0 fusion.112
  100.2 2.5 fusion.111
  104.0 1.2 multiply_reduce_fusion.10
  105.5 2.0 fusion.112
  111.2 2.5 fusion.111
  115.0 1.2 multiply_reduce_fusion.10
  116.5 2.0 fusion.112
  122.2 2.5 fusion.111
  126.0 1.2 multiply_reduce_fusion.10
  127.4 2.0 fusion.112
  133.2 2.5 fusion.111
  137.0 1.2 multiply_reduce_fusion.10
  138.4 2.0 fusion.112
  144.2 2.5 fusion.111
  147.9 1.2 multiply_reduce_fusion.10
  149.4 2.0 fusion.112
  152.6 106.6 %while.27 = (s32[]{:T(128)}, f32[192,2048]{1,0:T(8,128)S(1)}, f32[192,32]{1,0:T(8,128)S(1)}, f32[192]{0:T(256)S(1)}, bf16[8,24,2048]{2,1,0:T(8,128)(2,1)}, /*ind...) while((s32[]{:T(128)}, f32[192,2048]{1,0:T(8,128)S(1)}, ...), condition=%wide.region_11.12_spmd, body=%wide.region_6.11_spmd.sunk | while | flops 313785664 | bytes 12832803 | solution.py:130
  155.5 1.6 fusion.101
  158.5 1.2 multiply_reduce_fusion.8
  159.9 1.3 convert_reduce_fusion.3
  161.6 2.0 convolution_bitcast_fusion.3
  168.9 1.6 fusion.101
  171.8 1.2 multiply_reduce_fusion.8
  173.2 1.3 convert_reduce_fusion.3
  174.9 2.0 convolution_bitcast_fusion.3
  182.2 1.6 fusion.101
  185.1 1.2 multiply_reduce_fusion.8
  186.6 1.3 convert_reduce_fusion.3
  188.2 2.0 convolution_bitcast_fusion.3
  195.5 1.6 fusion.101
  198.4 1.2 multiply_reduce_fusion.8
  199.9 1.3 convert_reduce_fusion.3
  201.5 2.0 convolution_bitcast_fusion.3
  208.8 1.6 fusion.101
  211.7 1.2 multiply_reduce_fusion.8
  213.2 1.3 convert_reduce_fusion.3
  214.9 2.0 convolution_bitcast_fusion.3
  222.1 1.6 fusion.101
  225.0 1.2 multiply_reduce_fusion.8
  226.5 1.3 convert_reduce_fusion.3
  228.2 2.0 convolution_bitcast_fusion.3
  235.4 1.6 fusion.101
  238.3 1.2 multiply_reduce_fusion.8
  239.8 1.3 convert_reduce_fusion.3
  241.5 2.0 convolution_bitcast_fusion.3
  248.7 1.6 fusion.101
  251.6 1.2 multiply_reduce_fusion.8
  253.1 1.3 convert_reduce_fusion.3
  254.8 2.0 convolution_bitcast_fusion.3
  260.4 73.8 %all-reduce = (f32[192,32]{1,0:T(8,128)S(1)}, f32[192]{0:T(256)S(1)}) all-reduce(f32[192,32]{1,0:T(8,128)S(1)} %get-tuple-element.117, f32[192]{0:T(256)S(1)} %get-tuple-element.118), channel_id=1, replica_groups=mesh['grp'=8,'dev'=32] {'grp','dev'}, use_global_device_ids=true, to_apply=%region_13.14 | all-reduce | flops 6336 | bytes 50688 | tf_op jit(solution)/shard_map/psum | solution.py:134
  335.1 182.2 %all-reduce.3.cloned.1.call-done = f32[192,2048]{1,0:T(8,128)} async-done(((f32[192,2048]{1,0:T(8,128)}), f32[192,2048]{1,0:T(8,128)}) %all-reduce.3.cloned.1.call-update) | async-done | bytes 1572880 | tf_op jit(solution)/shard_map/psum | solution.py:134
  517.3 1.5 dynamic-slice_divide_fusion
  (309 shorter events, 92.4 us)
Async XLA Ops:
  7.2 55.2 %copy-start = (f32[64,32]{0,1:T(8,128)S(1)}, f32[64,32]{0,1:T(8,128)}, u32[]{:S(2)}) copy-start(f32[64,32]{0,1:T(8,128)} %param.13) | copy-start | bytes 24580
  7.2 56.1 %copy-start.2 = (bf16[2048,256]{1,0:T(8,128)(2,1)S(1)}, bf16[2048,256]{1,0:T(8,128)(2,1)}, u32[]{:S(2)}) copy-start(bf16[2048,256]{1,0:T(8,128)(2,1)} %param.11) | copy-start | bytes 3145732
  7.2 57.3 %copy-start.3 = (f32[192]{0:T(256)S(1)}, f32[192]{0:T(256)}, u32[]{:S(2)}) copy-start(f32[192]{0:T(256)} %param.15) | copy-start | bytes 2308
  7.2 510.1 %all-reduce.3.cloned.1.call-start = ((), (), s32[]{:S(2)}) async-start(), calls=%async_computation | async-start | bytes 3145728 | tf_op jit(solution)/shard_map/psum | solution.py:134
  259.2 1.1 copy-start.1
Sparse Core Ops, SparseCore 0:
  260.5 256.7 all-reduce.2
where the time goes:
time: 528 us; the launch traced here: 526 us
  waiting for transfers between devices  182 us (34%)
  blocking collectives  128 us (24%)
  matrix products  82.1 us (16%)
  local copies, waits for them, and re-layouts  64.7 us (12%)
  other arithmetic  42.8 us (8%)
  between operations  14.2 us (3%)
  loops' own time  12.1 us (2%)
    psum x1, waiting for transfers between devices, local(): merged = lax.psum((numer_all, cycles_all, mass_all), ('grp', 'dev'))  182 us
    psum x1, blocking collectives, local(): merged = lax.psum((numer_all, cycles_all, mass_all), ('grp', 'dev'))  73.8 us
    all_gather x1, blocking collectives, local(): gathered = lax.all_gather(references, 'dev', axis=0, tiled=True)  53.8 us
    dot_general x16, matrix products, block_scores(): jnp.einsum('pkmc,mcb->pmkb', stacked, weighted, preferred_element_type=jn...  32.7 us
    dot_general x16, matrix products, block_scores(): jnp.einsum('pmkb,pmr->krb', crossed, score_table, preferred_element_type=...  26.3 us
    dynamic_slice x32, local copies, waits for them, and re-layouts, local(): lax.scan(one_block, initial, (blocks, jnp.arange(block_count, dtype=jnp.i...  23.9 us
    reduce_sum x16, other arithmetic, class_rows(): jnp.sum(squares, axis=2) * factor[None, :, None]  18.6 us
    dot_general x8, matrix products, one_block(): jnp.einsum('pmkb,mcb->kpmc', spectra, weighted, preferred_element_type=jn...  15.7 us
  transfers between devices with their start and end apart: 1, of which 1 were waited for; matrix products, arithmetic and copies ran while one was open for 0% of the time, Pallas kernels for 0%

commit v1 on v0

--- a/solution.py
+++ b/solution.py
@@ -131,7 +131,7 @@
         one_block, empty_sums, (blocks, jnp.arange(block_count, dtype=jnp.int32))
     )
     numer_all, cycles_all, mass_all = result
-    merged = lax.psum((numer_all, cycles_all, mass_all), ("grp", "dev"))
+    merged = lax.psum(lax.psum((numer_all, cycles_all, mass_all), "dev"), "grp")
     own_start = lax.axis_index("dev") * CLS_DEV
     numerator = lax.dynamic_slice_in_dim(merged[0], own_start, CLS_DEV, 0)
     cycle_sum = lax.dynamic_slice_in_dim(merged[1], own_start, CLS_DEV, 0)

time: 528 us -> 585 us (1.11)
  blocking collectives: 128 us -> 216 us
  waiting for transfers between devices: 182 us -> 149 us
    psum x1 -> x2, blocking collectives: 73.8 us -> 163 us  [local(): merged = lax.psum(lax.psum((numer_all, cycles_all, mass_all), 'dev'), 'grp')]
    psum x1 -> x2, waiting for transfers between devices: 182 us -> 149 us  [local(): merged = lax.psum(lax.psum((numer_all, cycles_all, mass_all), 'dev'), 'grp')]
  transfers between devices with their start and end apart: 1 -> 2, of which waited for: 1 -> 1; matrix products, arithmetic and copies ran while one was open for 0% -> 0% of each run, Pallas kernels for 0% -> 0%
where the time goes in v1:
time: 585 us; the launch traced here: 581 us
  blocking collectives  216 us (37%)
  waiting for transfers between devices  149 us (25%)
  matrix products  82.1 us (14%)
  local copies, waits for them, and re-layouts  64.6 us (11%)
  other arithmetic  42.8 us (7%)
  between operations  14.2 us (2%)
  loops' own time  12.1 us (2%)
    psum x2, blocking collectives, local(): merged = lax.psum(lax.psum((numer_all, cycles_all, mass_all), 'dev'), 'grp')  163 us
    psum x2, waiting for transfers between devices, local(): merged = lax.psum(lax.psum((numer_all, cycles_all, mass_all), 'dev'), 'grp')  149 us
    all_gather x1, blocking collectives, local(): gathered = lax.all_gather(references, 'dev', axis=0, tiled=True)  53.8 us
    dot_general x16, matrix products, block_scores(): jnp.einsum('pkmc,mcb->pmkb', stacked, weighted, preferred_element_type=jn...  32.7 us
    dot_general x16, matrix products, block_scores(): jnp.einsum('pmkb,pmr->krb', crossed, score_table, preferred_element_type=...  26.3 us
    dynamic_slice x32, local copies, waits for them, and re-layouts, local(): lax.scan(one_block, initial, (blocks, jnp.arange(block_count, dtype=jnp.i...  23.9 us
    reduce_sum x16, other arithmetic, class_rows(): jnp.sum(squares, axis=2) * factor[None, :, None]  18.6 us
    dot_general x8, matrix products, one_block(): jnp.einsum('pmkb,mcb->kpmc', spectra, weighted, preferred_element_type=jn...  15.7 us
  transfers between devices with their start and end apart: 2, of which 1 were waited for; matrix products, arithmetic and copies ran while one was open for 0% of the time, Pallas kernels for 0%

profile of v1, /device:TPU:2, one launch (start us, length us, event | category | flops | bytes accessed | tf_op | source)
XLA Modules:
  0.0 581.2 jit_solution(14412001032394564507)
XLA Ops:
  7.5 53.8 %all-gather = bf16[32,6,2048]{2,1,0:T(8,128)(2,1)S(1)} all-gather(bf16[1,6,2048]{2,1,0:T(8,128)(2,1)} %bitcast.179), channel_id=1, replica_groups=mesh['grp'=8,'dev'=32] {'dev'}, dimensions={0}, use_global_device_ids=true | all-gather | bytes 811008 | tf_op jit(solution)/shard_map/all_gather | solution.py:85
  61.2 1.2 reshape.224
  63.3 1.2 fusion.39
  64.5 87.8 %while.28 = (s32[]{:T(128)}, f32[256]{0:T(256)S(1)}, f32[256]{0:T(256)S(1)}, bf16[8,24,2048]{2,1,0:T(8,128)(2,1)}, bf16[32,64,256]{2,1,0:T(8,128)(2,1)}, /*index...) while((s32[]{:T(128)}, f32[256]{0:T(256)S(1)}, ...), condition=%wide.region_5.6_spmd.clone, body=%wide.region_0.5_spmd.clone.sunk | while | flops 159947328 | bytes 10727242 | solution.py:98
  67.3 2.5 fusion.111
  71.1 1.2 multiply_reduce_fusion.10
  72.5 2.0 fusion.112
  78.3 2.5 fusion.111
  82.0 1.2 multiply_reduce_fusion.10
  83.5 2.0 fusion.112
  89.2 2.5 fusion.111
  93.0 1.2 multiply_reduce_fusion.10
  94.5 2.0 fusion.112
  100.2 2.5 fusion.111
  104.0 1.2 multiply_reduce_fusion.10
  105.5 2.0 fusion.112
  111.2 2.5 fusion.111
  115.0 1.2 multiply_reduce_fusion.10
  116.5 2.0 fusion.112
  122.2 2.5 fusion.111
  126.0 1.2 multiply_reduce_fusion.10
  127.4 2.0 fusion.112
  133.2 2.5 fusion.111
  137.0 1.2 multiply_reduce_fusion.10
  138.4 2.0 fusion.112
  144.2 2.5 fusion.111
  147.9 1.2 multiply_reduce_fusion.10
  149.4 2.0 fusion.112
  152.6 106.6 %while.27 = (s32[]{:T(128)}, f32[192,2048]{1,0:T(8,128)S(1)}, f32[192,32]{1,0:T(8,128)S(1)}, f32[192]{0:T(256)S(1)}, bf16[8,24,2048]{2,1,0:T(8,128)(2,1)}, /*ind...) while((s32[]{:T(128)}, f32[192,2048]{1,0:T(8,128)S(1)}, ...), condition=%wide.region_11.12_spmd, body=%wide.region_6.11_spmd.sunk | while | flops 313785664 | bytes 12832803 | solution.py:130
  155.5 1.6 fusion.101
  158.5 1.2 multiply_reduce_fusion.8
  159.9 1.3 convert_reduce_fusion.3
  161.6 2.0 convolution_bitcast_fusion.3
  168.9 1.6 fusion.101
  171.8 1.2 multiply_reduce_fusion.8
  173.2 1.3 convert_reduce_fusion.3
  174.9 2.0 convolution_bitcast_fusion.3
  182.2 1.6 fusion.101
  185.1 1.2 multiply_reduce_fusion.8
  186.6 1.3 convert_reduce_fusion.3
  188.2 2.0 convolution_bitcast_fusion.3
  195.5 1.6 fusion.101
  198.4 1.2 multiply_reduce_fusion.8
  199.9 1.3 convert_reduce_fusion.3
  201.5 2.0 convolution_bitcast_fusion.3
  208.8 1.6 fusion.101
  211.7 1.2 multiply_reduce_fusion.8
  213.2 1.3 convert_reduce_fusion.3
  214.9 2.0 convolution_bitcast_fusion.3
  222.1 1.6 fusion.101
  225.0 1.2 multiply_reduce_fusion.8
  226.5 1.3 convert_reduce_fusion.3
  228.2 2.0 convolution_bitcast_fusion.3
  235.4 1.6 fusion.101
  238.3 1.2 multiply_reduce_fusion.8
  239.8 1.3 convert_reduce_fusion.3
  241.5 2.0 convolution_bitcast_fusion.3
  248.7 1.6 fusion.101
  253.1 1.3 convert_reduce_fusion.3
  254.8 2.0 convolution_bitcast_fusion.3
  260.4 148.8 %all-reduce.5.cloned.1.call-done = f32[192,2048]{1,0:T(8,128)} async-done(((f32[192,2048]{1,0:T(8,128)}), f32[192,2048]{1,0:T(8,128)}) %all-reduce.5.cloned.1.call-update) | async-done | bytes 1572880 | tf_op jit(solution)/shard_map/psum | solution.py:134
  409.3 140.5 %all-reduce = (f32[192,32]{1,0:T(8,128)S(1)}, f32[192]{0:T(256)S(1)}) all-reduce(f32[192,32]{1,0:T(8,128)S(1)} %get-tuple-element.117, f32[192]{0:T(256)S(1)} %get-tuple-element.118), channel_id=1, replica_groups=mesh['grp'=8,'dev'=32] {'dev'}, use_global_device_ids=true, to_apply=%region_14.15 | all-reduce | flops 6336 | bytes 50688 | tf_op jit(solution)/shard_map/psum | solution.py:134
  549.7 22.2 %all-reduce.1 = (f32[192,32]{1,0:T(8,128)S(1)}, f32[192]{0:T(256)S(1)}) all-reduce(f32[192,32]{1,0:T(8,128)S(1)} %get-tuple-element.193, f32[192]{0:T(256)S(1)} %get-tuple-element.194), channel_id=1, replica_groups=mesh['grp'=8,'dev'=32] {'grp'}, use_global_device_ids=true, to_apply=%region_15.16 | all-reduce | flops 6336 | bytes 50688 | tf_op jit(solution)/shard_map/psum | solution.py:134
  572.9 1.5 dynamic-slice_divide_fusion
  (313 shorter events, 93.6 us)
Async XLA Ops:
  7.2 55.2 %copy-start = (f32[64,32]{0,1:T(8,128)S(1)}, f32[64,32]{0,1:T(8,128)}, u32[]{:S(2)}) copy-start(f32[64,32]{0,1:T(8,128)} %param.13) | copy-start | bytes 24580
  7.2 56.1 %copy-start.2 = (bf16[2048,256]{1,0:T(8,128)(2,1)S(1)}, bf16[2048,256]{1,0:T(8,128)(2,1)}, u32[]{:S(2)}) copy-start(bf16[2048,256]{1,0:T(8,128)(2,1)} %param.11) | copy-start | bytes 3145732
  7.2 57.3 %copy-start.3 = (f32[192]{0:T(256)S(1)}, f32[192]{0:T(256)}, u32[]{:S(2)}) copy-start(f32[192]{0:T(256)} %param.15) | copy-start | bytes 2308
  7.2 402.0 %all-reduce.5.cloned.1.call-start = ((), (), s32[]{:S(2)}) async-start(), calls=%async_computation | async-start | bytes 3145728 | tf_op jit(solution)/shard_map/psum | solution.py:134
  259.2 1.1 copy-start.1
  260.4 312.5 %all-reduce.7.cloned.1.call-start = ((), (), s32[]{:S(2)}) async-start(), calls=%async_computation.1 | async-start | bytes 3145728 | tf_op jit(solution)/shard_map/psum | solution.py:134
Sparse Core Ops, SparseCore 0:
  260.5 148.6 all-reduce.4
  411.7 63.9 all-reduce.6
